TPU v7x, 512 devices: a whole 4x8x8 slice. The times are simulated.
512 devices in a mesh: section: 8 (over y), dp: 64 (over x, z, core).
Axes of the slice: x: 4, y: 8, z: 8, core: 2. Of those that a mesh axis runs over, the one named last changes fastest.
Arguments:
- queries: bfloat16 [65536, 3584], P(('section', 'dp')), may hold values from -1 to 1
- passages: bfloat16 [128, 64, 3584], P('dp'), may hold values from -1 to 1
- candidates: int32 [512, 3], P('section'), may hold values from 0 to 63, as said below
- counts: int32 [512], P('section'), may hold values from 1 to 3, 1024 in all
- teacher: float32 [65536, 384], P(('section', 'dp')), may hold values from -20 to 450
- section_weights: bfloat16 [8, 3584, 3584], P('section', 'dp'), may hold values from -0.09375 to 0.09375
- section_inputs: bfloat16 [8, 64, 3584], P('section', None, 'dp'), may hold values from -1.5 to 1.5
- pre_acts: bfloat16 [8, 64, 3584], P('section', None, 'dp'), may hold values from -8 to 8
Outputs:
- query_grads: bfloat16 [65536, 3584], P(('section', 'dp'))
- passage_grads: bfloat16 [128, 64, 3584], P('dp')
- grad_inputs: float32 [8, 64, 3584], P('section', None, 'dp')
- weight_grads: bfloat16 [8, 3584, 3584], P('section', 'dp')
Inputs may be any that keep to these rules, and one draw needn't show every extreme that they name: `candidates`: each row names 3 different passage blocks. A query block uses the first counts[b] entries of its row of candidates.
All inputs are finite; a program needn't handle non-finite values.
Results may differ from a plain program's by a relative error of at most 0.0085.
Values may be sent and summed in bfloat16 or wider, within the bound.
No kernel may reach another device: no remote copies, remote signals or barrier semaphores. Data moves between devices by JAX's collectives and lax.ppermute only.
A program may use at most 64 MiB of HBM per device.

v0:
```python
import jax
import jax.numpy as jnp
from jax import lax
from jax.sharding import PartitionSpec as P

INVERSE_TEMP = 20.0


def passed_along(value, axis, steps):
    count = lax.axis_size(axis)
    initial, last = (max(0, -steps), min(count, count - steps))
    return lax.ppermute(value, axis, [(source, source + steps) for source in range(initial, last)])


def soft_weights(logits, valid):
    masked = jnp.where(valid, logits, -1e30)
    highest = jnp.max(masked, axis=-1, keepdims=True)
    expons = jnp.where(valid, jnp.exp(masked - highest), 0.0)
    return expons / jnp.sum(expons, axis=-1, keepdims=True)


def body(queries, passages, candidates, counts, teacher, section_weights, section_inputs, pre_acts):
    dp_count = lax.axis_size("dp")
    dp_index = lax.axis_index("dp")
    stripe, block_total, width = passages.shape
    row_block_count = stripe * dp_count
    blocks_here = candidates.shape[0] // dp_count
    slot_count = candidates.shape[1]
    requests = blocks_here * slot_count
    all_slots = candidates.reshape(-1)
    outgoing = jnp.take(passages, all_slots, axis=1)
    pulled_rows = lax.all_to_all(outgoing, "dp", split_axis=1, concat_axis=0, tiled=True)
    pulled_rows = pulled_rows.reshape(row_block_count, blocks_here, slot_count, width)
    own_counts = lax.dynamic_slice_in_dim(counts, dp_index * blocks_here, blocks_here)
    slot_valid = jnp.arange(slot_count, dtype=jnp.int32)[None, :] < own_counts[:, None]
    column_valid = jnp.repeat(slot_valid, row_block_count, axis=1)[:, None, :]
    query_row_items = queries.reshape(blocks_here, row_block_count, width)
    logits = (
        jnp.einsum(
            "ixp,wifp->ixfw", query_row_items, pulled_rows, preferred_element_type=jnp.float32
        )
        * INVERSE_TEMP
    )
    logits = logits.reshape(blocks_here, row_block_count, slot_count * row_block_count)
    target_logits = soft_weights(
        teacher.reshape(blocks_here, row_block_count, slot_count * row_block_count), column_valid
    )
    weight_matrices = (soft_weights(logits, column_valid) - target_logits).astype(jnp.bfloat16)
    weight_matrices = weight_matrices.reshape(
        blocks_here, row_block_count, slot_count, row_block_count
    )
    query_sums = (
        jnp.einsum(
            "geal,lgay->gey", weight_matrices, pulled_rows, preferred_element_type=jnp.float32
        )
        * INVERSE_TEMP
    )
    passage_sums = (
        jnp.einsum(
            "fnyw,fnj->wfyj", weight_matrices, query_row_items, preferred_element_type=jnp.float32
        )
        * INVERSE_TEMP
    )
    block_terms = passage_sums.reshape(row_block_count, requests, width).astype(jnp.bfloat16)
    micro_count = section_inputs.shape[1] // dp_count
    col_width = width // dp_count
    micro_cols = jnp.transpose(
        query_sums[0, :micro_count].reshape(micro_count, dp_count, col_width), (1, 0, 2)
    )
    incoming_piece = lax.all_to_all(block_terms, "dp", split_axis=0, concat_axis=1, tiled=True)
    entry = lax.all_to_all(micro_cols, "dp", split_axis=0, concat_axis=1, tiled=True)
    onehot = (all_slots[:, None] == jnp.arange(block_total, dtype=jnp.int32)[None, :]).astype(
        jnp.float32
    )
    dense = jnp.einsum(
        "sjd,jn->snd",
        incoming_piece.astype(jnp.float32),
        onehot,
        precision=lax.Precision.HIGHEST,
        preferred_element_type=jnp.float32,
    )
    passage_out = lax.psum(dense, "section").astype(jnp.bfloat16)
    weight_rows = section_weights[0]
    input_cols = section_inputs[0]
    pre = pre_acts[0].astype(jnp.float32)
    sigma = jax.nn.sigmoid(pre)
    slope = sigma * (1.0 + pre * (1.0 - sigma))
    carry = entry.reshape(dp_count * micro_count, col_width)
    section_count = lax.axis_size("section")
    section_index = lax.axis_index("section")
    grad_cols = jnp.zeros_like(carry)
    grad_weight = jnp.zeros((col_width, width), jnp.float32)
    for section_turn in range(section_count):
        active_flag = section_count - 1 - section_turn
        inner = (carry * slope).astype(jnp.bfloat16)
        piece = lax.all_gather(inner, "dp", axis=1, tiled=True)
        back_sum = jnp.einsum("mj,ij->mi", piece, weight_rows, preferred_element_type=jnp.float32)
        weight_part = jnp.einsum("mi,mj->ij", input_cols, piece, preferred_element_type=jnp.float32)
        back_sum, layer_weight = (back_sum, weight_part)
        updated = carry + back_sum
        is_active = section_index == active_flag
        grad_cols = jnp.where(is_active, updated, grad_cols)
        grad_weight = jnp.where(is_active, layer_weight, grad_weight)
        if section_turn + 1 < section_count:
            carry = passed_along(updated, "section", -1)
    return (
        query_sums.reshape(blocks_here * row_block_count, width).astype(jnp.bfloat16),
        passage_out,
        grad_cols[None],
        grad_weight[None].astype(jnp.bfloat16),
    )


def solution(mesh):
    placed = (
        P(("section", "dp"), None),
        P("dp", None, None),
        P("section", None),
        P("section"),
        P(("section", "dp"), None),
        P("section", "dp", None),
        P("section", None, "dp"),
        P("section", None, "dp"),
    )
    return jax.shard_map(
        body,
        mesh=mesh,
        in_specs=placed,
        out_specs=(
            P(("section", "dp"), None),
            P("dp", None, None),
            P("section", None, "dp"),
            P("section", "dp", None),
        ),
        check_vma=False,
    )
```

profile of v0, /device:TPU:16, one launch (start us, length us, event | category | flops | bytes accessed | tf_op | source)
XLA Modules:
  0.0 732.7 jit_solution(10540011991136659404)
XLA Ops:
  0.6 0.9 copy.27
  1.6 0.1 reshape.238
  1.8 15.2 %gather_fusion = bf16[192,2,3584]{2,0,1:T(8,128)(2,1)} fusion(bf16[2,64,3584]{2,1,0:T(8,128)(2,1)} %param.9, s32[1024]{0:T(1024)S(1)} %pad_clamp_fusion), kind=kCustom, calls=%fused_computation | custom fusion | bytes 5505792 | tf_op jit(solution)/shard_map/jit(_take)/gather | solution.py:31
  17.0 2.1 select_bitcast_fusion
  19.1 4.4 copy.29
  23.5 14.1 %all-to-all-start = ((bf16[2,192,3584]{2,0,1:T(2,128)(2,1)}), bf16[2,192,3584]{2,0,1:T(2,128)(2,1)}, u32[]{:S(2)}, u32[]{:S(2)}) async-start(bf16[2,192,3584]{2,0,1:T(2,128)(2,1)} %copy.29), calls=%async_computation | async-start | bytes 5505024 | tf_op jit(solution)/shard_map/all_to_all | solution.py:32
  37.8 0.6 dynamic_slice.3
  38.4 0.6 iota_compare_fusion.1
  39.2 0.1 select_reduce_fusion
  39.3 0.1 fusion.29
  39.5 62.7 %all-to-all-done = bf16[2,192,3584]{2,0,1:T(2,128)(2,1)} async-done(((bf16[2,192,3584]{2,0,1:T(2,128)(2,1)}), bf16[2,192,3584]{2,0,1:T(2,128)(2,1)}, u32[]{:S(2)}, u32[]{:S(2)}) %all-to-all-start) | async-done | bytes 2752544 | tf_op jit(solution)/shard_map/all_to_all | solution.py:32
  102.2 5.2 copy.30
  107.4 6.8 reshape.239
  114.2 2.8 fusion.27
  117.0 0.1 fusion.21
  117.2 0.2 fusion.28
  117.4 1.6 fusion.47
  119.0 0.7 transpose_reshape_squeeze.3
  119.7 6.2 all-to-all-start.2
  125.9 0.9 fusion.1
  126.7 4.2 copy.33
  131.0 4.3 all-to-all-done.2
  135.3 6.4 all-to-all-start.1
  141.8 124.8 %all_gather.24 = bf16[64,3584]{0,1:T(8,128)(2,1)S(1)} all-gather(bf16[64,56]{0,1:T(8,128)(2,1)S(1)} %fusion.38), channel_id=1, replica_groups=mesh['section'=8,'dp'=64] {'dp'}, dimensions={1}, use_global_device_ids=true | all-gather | bytes 465920 | tf_op jit(solution)/shard_map/all_gather | solution.py:96
  266.6 0.3 convolution_add_fusion.7
  266.9 2.8 collective-permute-start
  269.7 0.7 convolution_select_fusion
  270.4 2.3 collective-permute-done
  272.7 49.7 %all_gather.25 = bf16[64,3584]{0,1:T(8,128)(2,1)S(1)} all-gather(bf16[64,56]{0,1:T(8,128)(2,1)S(1)} %multiply_convert_fusion.6), channel_id=1, replica_groups=mesh['section'=8,'dp'=64] {'dp'}, dimensions={1}, use_global_device_ids=true | all-gather | bytes 465920 | tf_op jit(solution)/shard_map/all_gather | solution.py:96
  322.4 0.3 convolution_add_fusion.6
  322.7 2.8 collective-permute-start.1
  325.5 0.7 convolution_select_fusion.1
  326.2 2.9 collective-permute-done.1
  329.1 48.2 %all_gather.26 = bf16[64,3584]{0,1:T(8,128)(2,1)S(1)} all-gather(bf16[64,56]{0,1:T(8,128)(2,1)S(1)} %multiply_convert_fusion.5), channel_id=1, replica_groups=mesh['section'=8,'dp'=64] {'dp'}, dimensions={1}, use_global_device_ids=true | all-gather | bytes 465920 | tf_op jit(solution)/shard_map/all_gather | solution.py:96
  377.3 0.3 convolution_add_fusion.5
  377.6 2.2 collective-permute-start.2
  379.8 0.7 convolution_select_fusion.2
  380.5 4.1 collective-permute-done.2
  384.6 50.1 %all_gather.27 = bf16[64,3584]{0,1:T(8,128)(2,1)S(1)} all-gather(bf16[64,56]{0,1:T(8,128)(2,1)S(1)} %multiply_convert_fusion.4), channel_id=1, replica_groups=mesh['section'=8,'dp'=64] {'dp'}, dimensions={1}, use_global_device_ids=true | all-gather | bytes 465920 | tf_op jit(solution)/shard_map/all_gather | solution.py:96
  434.7 0.3 convolution_add_fusion.4
  435.0 1.9 collective-permute-start.3
  436.9 0.7 convolution_select_fusion.3
  437.6 4.4 collective-permute-done.3
  442.0 48.2 %all_gather.28 = bf16[64,3584]{0,1:T(8,128)(2,1)S(1)} all-gather(bf16[64,56]{0,1:T(8,128)(2,1)S(1)} %multiply_convert_fusion.3), channel_id=1, replica_groups=mesh['section'=8,'dp'=64] {'dp'}, dimensions={1}, use_global_device_ids=true | all-gather | bytes 465920 | tf_op jit(solution)/shard_map/all_gather | solution.py:96
  490.2 0.3 convolution_add_fusion.3
  490.5 1.9 collective-permute-start.4
  492.4 0.7 convolution_select_fusion.4
  493.1 4.4 collective-permute-done.4
  497.5 49.7 %all_gather.29 = bf16[64,3584]{0,1:T(8,128)(2,1)S(1)} all-gather(bf16[64,56]{0,1:T(8,128)(2,1)S(1)} %multiply_convert_fusion.2), channel_id=1, replica_groups=mesh['section'=8,'dp'=64] {'dp'}, dimensions={1}, use_global_device_ids=true | all-gather | bytes 465920 | tf_op jit(solution)/shard_map/all_gather | solution.py:96
  547.2 0.3 convolution_add_fusion.2
  547.4 1.9 collective-permute-start.5
  549.4 0.7 convolution_select_fusion.5
  550.0 4.4 collective-permute-done.5
  554.5 48.3 %all_gather.30 = bf16[64,3584]{0,1:T(8,128)(2,1)S(1)} all-gather(bf16[64,56]{0,1:T(8,128)(2,1)S(1)} %multiply_convert_fusion.1), channel_id=1, replica_groups=mesh['section'=8,'dp'=64] {'dp'}, dimensions={1}, use_global_device_ids=true | all-gather | bytes 465920 | tf_op jit(solution)/shard_map/all_gather | solution.py:96
  602.8 0.3 convolution_add_fusion.1
  603.1 1.9 collective-permute-start.6
  605.0 0.7 convolution_select_fusion.6
  605.7 4.4 collective-permute-done.6
  610.1 49.7 %all_gather.31 = bf16[64,3584]{0,1:T(8,128)(2,1)S(1)} all-gather(bf16[64,56]{0,1:T(8,128)(2,1)S(1)} %multiply_convert_fusion), channel_id=1, replica_groups=mesh['section'=8,'dp'=64] {'dp'}, dimensions={1}, use_global_device_ids=true | all-gather | bytes 465920 | tf_op jit(solution)/shard_map/all_gather | solution.py:96
  659.8 1.4 fusion.4
  661.2 0.9 fusion.7
  662.1 4.4 copy.34
  666.5 0.6 convolution_bitcast_fusion
  667.1 65.4 %all-reduce.1 = bf16[2,64,3584]{2,1,0:T(8,128)(2,1)} all-reduce(f32[2,64,3584]{2,1,0:T(8,128)S(1)} %convolution_bitcast_fusion), channel_id=1, replica_groups=mesh['section'=8,'dp'=64] {'section'}, use_global_device_ids=true, to_apply=%region_4.5 | all-reduce | flops 458752 | bytes 2752512 | tf_op jit(solution)/shard_map/psum | solution.py:82
  (31 shorter events, 0.7 us)
Async XLA Ops:
  0.6 113.6 %copy-start = (bf16[128,3584]{1,0:T(8,128)(2,1)S(1)}, bf16[128,3584]{1,0:T(8,128)(2,1)}, u32[]{:S(2)}) copy-start(bf16[128,3584]{1,0:T(8,128)(2,1)} %param.8) | copy-start | bytes 2752516
  23.5 14.2 %copy-start.5 = (f32[128,384]{1,0:T(8,128)S(1)}, f32[128,384]{1,0:T(8,128)}, u32[]{:S(2)}) copy-start(f32[128,384]{1,0:T(8,128)} %param.12) | copy-start | bytes 589828
  23.5 14.3 %copy-start.6 = (s32[64]{0:T(128)S(1)}, s32[64]{0:T(128)}, u32[]{:S(2)}) copy-start(s32[64]{0:T(128)} %param.11) | copy-start | bytes 772
  23.5 78.7 %all-to-all-start = ((bf16[2,192,3584]{2,0,1:T(2,128)(2,1)}), bf16[2,192,3584]{2,0,1:T(2,128)(2,1)}, u32[]{:S(2)}, u32[]{:S(2)}) async-start(bf16[2,192,3584]{2,0,1:T(2,128)(2,1)} %copy.29), calls=%async_computation | async-start | bytes 5505024 | tf_op jit(solution)/shard_map/all_to_all | solution.py:32
  114.2 3.1 copy-start.1
  119.7 15.6 %all-to-all-start.2 = ((f32[64,1,56]{2,1,0:T(1,128)}), f32[64,1,56]{2,1,0:T(1,128)S(1)}, u32[]{:S(2)}, u32[]{:S(2)}) async-start(f32[64,1,56]{2,1,0:T(1,128)} %bitcast.24), calls=%async_computation.2 | async-start | bytes 65536 | tf_op jit(solution)/shard_map/all_to_all | solution.py:71
  131.0 10.8 %copy-start.4 = (bf16[1,64,56]{1,2,0:T(8,128)(2,1)S(1)}, bf16[1,64,56]{1,2,0:T(8,128)(2,1)}, u32[]{:S(2)}) copy-start(bf16[1,64,56]{1,2,0:T(8,128)(2,1)} %param.15) | copy-start | bytes 21508
  131.0 135.7 %copy-start.2 = (bf16[1,56,3584]{2,1,0:T(8,128)(2,1)S(1)}, bf16[1,56,3584]{2,1,0:T(8,128)(2,1)}, u32[]{:S(2)}) copy-start(bf16[1,56,3584]{2,1,0:T(8,128)(2,1)} %param.13) | copy-start | bytes 1204228
  131.0 138.8 %copy-start.3 = (bf16[1,64,56]{1,2,0:T(8,128)(2,1)S(1)}, bf16[1,64,56]{1,2,0:T(8,128)(2,1)}, u32[]{:S(2)}) copy-start(bf16[1,64,56]{1,2,0:T(8,128)(2,1)} %param.14) | copy-start | bytes 21508
  135.3 526.8 %all-to-all-start.1 = ((bf16[128,3,3584]{2,1,0:T(4,128)(2,1)}), bf16[128,3,3584]{2,1,0:T(4,128)(2,1)}, u32[]{:S(2)}, u32[]{:S(2)}) async-start(bf16[128,3,3584]{2,1,0:T(4,128)(2,1)} %copy.33), calls=%async_computation.1 | async-start | bytes 7340032 | tf_op jit(solution)/shard_map/all_to_all | solution.py:70
  266.9 5.8 collective-permute-start
  322.7 6.4 collective-permute-start.1
  377.6 7.0 collective-permute-start.2
  435.0 7.0 collective-permute-start.3
  490.5 7.0 collective-permute-start.4
  547.4 7.0 collective-permute-start.5
  603.1 7.0 collective-permute-start.6
where the time goes:
time: 742 us; the launch traced here: 733 us
  blocking collectives  534 us (72%)
  waiting for transfers between devices  93.9 us (13%)
  local copies, waits for them, and re-layouts  42.9 us (6%)
  starting transfers between devices  42.2 us (6%)
  matrix products  14.8 us (2%)
    all_gather x8, blocking collectives, body(): piece = lax.all_gather(inner, 'dp', axis=1, tiled=True)  469 us
    psum x1, blocking collectives, body(): passage_out = lax.psum(dense, 'section').astype(jnp.bfloat16)  65.4 us
    all_to_all x1, waiting for transfers between devices, body(): lax.all_to_all(outgoing, 'dp', split_axis=1, concat_axis=0, tiled=True)  62.7 us
    ppermute x7, waiting for transfers between devices, passed_along(): lax.ppermute(value, axis, [(source, source + steps) for source in range(i...  26.8 us
    ppermute x7, starting transfers between devices, passed_along(): lax.ppermute(value, axis, [(source, source + steps) for source in range(i...  15.5 us
    gather x1, local copies, waits for them, and re-layouts, body(): outgoing = jnp.take(passages, all_slots, axis=1)  15.2 us
  transfers between devices with their start and end apart: 10, of which 9 were waited for; matrix products, arithmetic and copies ran while one was open for 2% of the time, Pallas kernels for 0%

commit v1 on v0

--- a/solution.py
+++ b/solution.py
@@ -93,7 +93,8 @@
     for section_turn in range(section_count):
         active_flag = section_count - 1 - section_turn
         inner = (carry * slope).astype(jnp.bfloat16)
-        piece = lax.all_gather(inner, "dp", axis=1, tiled=True)
+        copies = jnp.concatenate([inner] * lax.axis_size("dp"), axis=1)
+        piece = lax.all_to_all(copies, "dp", 1, 1, tiled=True)
         back_sum = jnp.einsum("mj,ij->mi", piece, weight_rows, preferred_element_type=jnp.float32)
         weight_part = jnp.einsum("mi,mj->ij", input_cols, piece, preferred_element_type=jnp.float32)
         back_sum, layer_weight = (back_sum, weight_part)

time: 742 us -> 553 us (0.75)
  the two profiles are of different devices: /device:TPU:16 before, /device:TPU:30 now
where the time goes in v1:
time: 553 us; the launch traced here: 543 us
  blocking collectives  191 us (35%)
  waiting for transfers between devices  172 us (31%)
  local copies, waits for them, and re-layouts  89 us (16%)
  starting transfers between devices  57.2 us (10%)
  matrix products  26.2 us (5%)
    all_to_all x5, blocking collectives, body(): piece = lax.all_to_all(copies, 'dp', 1, 1, tiled=True)  110 us
    all_to_all x1, waiting for transfers between devices, body(): lax.all_to_all(block_terms, 'dp', split_axis=0, concat_axis=1, tiled=True)  66 us
    psum x1, blocking collectives, body(): passage_out = lax.psum(dense, 'section').astype(jnp.bfloat16)  65.2 us
    all_to_all x1, waiting for transfers between devices, body(): lax.all_to_all(outgoing, 'dp', split_axis=1, concat_axis=0, tiled=True)  61 us
    unnamed x531, local copies, waits for them, and re-layouts  46.8 us
    ppermute x7, waiting for transfers between devices, passed_along(): lax.ppermute(value, axis, [(source, source + steps) for source in range(i...  29.3 us
    all_to_all x3, starting transfers between devices, body(): piece = lax.all_to_all(copies, 'dp', 1, 1, tiled=True)  22 us
    all_to_all x1, blocking collectives, body(): lax.all_to_all(micro_cols, 'dp', split_axis=0, concat_axis=1, tiled=True)  15.4 us
  transfers between devices with their start and end apart: 12, of which 11 were waited for; matrix products, arithmetic and copies ran while one was open for 6% of the time, Pallas kernels for 0%

profile of v1, /device:TPU:30, one launch (start us, length us, event | category | flops | bytes accessed | tf_op | source)
XLA Modules:
  0.0 542.8 jit_solution(6778732099352030464)
XLA Ops:
  1.8 14.5 %gather_fusion = bf16[192,2,3584]{2,0,1:T(8,128)(2,1)} fusion(bf16[2,64,3584]{2,1,0:T(8,128)(2,1)} %param.9, s32[1024]{0:T(1024)S(1)} %pad_clamp_fusion), kind=kCustom, calls=%fused_computation | custom fusion | bytes 5505792 | tf_op jit(solution)/shard_map/jit(_take)/gather | solution.py:31
  16.4 2.1 select_bitcast_fusion
  18.5 4.4 copy.31
  22.9 14.3 %all-to-all-start = ((bf16[2,192,3584]{2,0,1:T(2,128)(2,1)}), bf16[2,192,3584]{2,0,1:T(2,128)(2,1)}, u32[]{:S(2)}, u32[]{:S(2)}) async-start(bf16[2,192,3584]{2,0,1:T(2,128)(2,1)} %copy.31), calls=%async_computation | async-start | bytes 5505024 | tf_op jit(solution)/shard_map/all_to_all | solution.py:32
  39.0 61.0 %all-to-all-done = bf16[2,192,3584]{2,0,1:T(2,128)(2,1)} async-done(((bf16[2,192,3584]{2,0,1:T(2,128)(2,1)}), bf16[2,192,3584]{2,0,1:T(2,128)(2,1)}, u32[]{:S(2)}, u32[]{:S(2)}) %all-to-all-start) | async-done | bytes 2752544 | tf_op jit(solution)/shard_map/all_to_all | solution.py:32
  99.9 5.2 copy.32
  105.2 6.8 %reshape.419 = bf16[128,3,3584]{2,0,1:T(8,128)(2,1)} reshape(bf16[64,2,3,3584]{3,1,0,2:T(2,128)(2,1)} %copy.32) | data formatting | bytes 5505024 | tf_op jit(solution)/shard_map/reshape.6
  111.9 2.8 fusion.27
  115.1 1.6 fusion.58
  116.8 15.4 %all_to_all.135 = f32[64,1,56]{2,1,0:T(1,128)S(1)} all-to-all(f32[64,1,56]{2,1,0:T(1,128)S(1)} %bitcast.260), channel_id=1, replica_groups=mesh['section'=8,'dp'=64] {'dp'}, dimensions={0} | all-to-all | bytes 28672 | tf_op jit(solution)/shard_map/all_to_all | solution.py:71
  133.0 21.1 %all_to_all.136 = bf16[64,2,1792]{2,1,0:T(2,128)(2,1)S(1)} all-to-all(bf16[64,2,1792]{2,1,0:T(2,128)(2,1)S(1)} %reshape.438), channel_id=1, replica_groups=mesh['section'=8,'dp'=64] {'dp'}, dimensions={0} | all-to-all | bytes 917504 | tf_op jit(solution)/shard_map/all_to_all | solution.py:97
  155.0 2.4 collective-permute-start
  157.4 4.6 collective-permute-done
  163.8 2.2 reshape.440
  166.0 22.2 %all_to_all.137 = bf16[64,2,1792]{2,1,0:T(2,128)(2,1)S(1)} all-to-all(bf16[64,2,1792]{2,1,0:T(2,128)(2,1)S(1)} %reshape.440), channel_id=1, replica_groups=mesh['section'=8,'dp'=64] {'dp'}, dimensions={0} | all-to-all | bytes 917504 | tf_op jit(solution)/shard_map/all_to_all | solution.py:97
  189.1 1.9 collective-permute-start.1
  191.0 5.0 collective-permute-done.1
  197.8 2.2 reshape.442
  200.0 22.1 %all_to_all.138 = bf16[64,2,1792]{2,1,0:T(2,128)(2,1)} all-to-all(bf16[64,2,1792]{2,1,0:T(2,128)(2,1)S(1)} %reshape.442), channel_id=1, replica_groups=mesh['section'=8,'dp'=64] {'dp'}, dimensions={0} | all-to-all | bytes 917504 | tf_op jit(solution)/shard_map/all_to_all | solution.py:97
  222.2 2.1 reshape.443
  224.6 1.9 collective-permute-start.2
  226.5 5.0 collective-permute-done.2
  233.3 2.8 reshape.444
  236.2 22.3 %all_to_all.139 = bf16[64,2,1792]{2,1,0:T(2,128)(2,1)} all-to-all(bf16[64,2,1792]{2,1,0:T(2,128)(2,1)} %reshape.444), channel_id=1, replica_groups=mesh['section'=8,'dp'=64] {'dp'}, dimensions={0} | all-to-all | bytes 917504 | tf_op jit(solution)/shard_map/all_to_all | solution.py:97
  258.5 2.8 reshape.445
  261.2 1.4 convolution_add_fusion.4
  262.7 1.9 collective-permute-start.3
  264.6 5.0 collective-permute-done.3
  271.5 2.8 reshape.446
  274.3 22.7 %all_to_all.140 = bf16[64,2,1792]{2,1,0:T(2,128)(2,1)} all-to-all(bf16[64,2,1792]{2,1,0:T(2,128)(2,1)} %reshape.446), channel_id=1, replica_groups=mesh['section'=8,'dp'=64] {'dp'}, dimensions={0} | all-to-all | bytes 917504 | tf_op jit(solution)/shard_map/all_to_all | solution.py:97
  297.0 2.8 reshape.447
  299.8 1.4 convolution_add_fusion.3
  301.2 1.9 collective-permute-start.4
  303.2 5.0 collective-permute-done.4
  309.1 0.9 copy-done.11
  310.0 2.8 reshape.448
  312.9 7.0 %all-to-all-start.8 = ((bf16[64,2,1792]{2,1,0:T(2,128)(2,1)}), bf16[64,2,1792]{2,1,0:T(2,128)(2,1)}, u32[]{:S(2)}, u32[]{:S(2)}) async-start(bf16[64,2,1792]{2,1,0:T(2,128)(2,1)} %reshape.448), calls=%async_computation.8 | async-start | bytes 917504 | tf_op jit(solution)/shard_map/all_to_all | solution.py:97
  320.7 4.1 copy.35
  324.9 10.3 %all-to-all-done.8 = bf16[64,2,1792]{2,1,0:T(2,128)(2,1)} async-done(((bf16[64,2,1792]{2,1,0:T(2,128)(2,1)}), bf16[64,2,1792]{2,1,0:T(2,128)(2,1)}, u32[]{:S(2)}, u32[]{:S(2)}) %all-to-all-start.8) | async-done | bytes 458784 | tf_op jit(solution)/shard_map/all_to_all | solution.py:97
  335.2 7.0 %all-to-all-start.1 = ((bf16[128,3,3584]{2,1,0:T(4,128)(2,1)}), bf16[128,3,3584]{2,1,0:T(4,128)(2,1)}, u32[]{:S(2)}, u32[]{:S(2)}) async-start(bf16[128,3,3584]{2,1,0:T(4,128)(2,1)} %copy.35), calls=%async_computation.1 | async-start | bytes 7340032 | tf_op jit(solution)/shard_map/all_to_all | solution.py:70
  342.2 2.8 reshape.449
  345.0 1.4 convolution_add_fusion.2
  346.4 1.9 collective-permute-start.5
  348.3 1.8 convolution_select_fusion
  350.2 3.2 collective-permute-done.5
  355.0 1.0 copy-done.12
  356.0 2.8 reshape.450
  358.8 66.0 %all-to-all-done.1 = bf16[128,3,3584]{2,1,0:T(4,128)(2,1)} async-done(((bf16[128,3,3584]{2,1,0:T(4,128)(2,1)}), bf16[128,3,3584]{2,1,0:T(4,128)(2,1)}, u32[]{:S(2)}, u32[]{:S(2)}) %all-to-all-start.1) | async-done | bytes 2752544 | tf_op jit(solution)/shard_map/all_to_all | solution.py:70
  424.9 8.1 %all-to-all-start.9 = ((bf16[64,2,1792]{2,1,0:T(2,128)(2,1)}), bf16[64,2,1792]{2,1,0:T(2,128)(2,1)}, u32[]{:S(2)}, u32[]{:S(2)}) async-start(bf16[64,2,1792]{2,1,0:T(2,128)(2,1)} %reshape.450), calls=%async_computation.9 | async-start | bytes 917504 | tf_op jit(solution)/shard_map/all_to_all | solution.py:97
  433.0 1.5 convolution_select_fusion.1
  434.5 1.4 convolution_select_fusion.2
  437.2 6.0 %copy.36 = bf16[64,2,3,3584]{3,1,2,0:T(2,128)(2,1)} copy(bf16[64,2,3,3584]{3,2,1,0:T(4,128)(2,1)} %bitcast.19) | data formatting | bytes 5505024 | tf_op jit(solution)/shard_map/all_to_all | solution.py:70
  443.2 5.1 all-to-all-done.9
  448.3 2.1 reshape.451
  450.7 1.9 collective-permute-start.6
  452.6 3.7 convolution_bitcast_fusion
  456.3 1.4 collective-permute-done.6
  459.5 2.9 reshape.452
  462.3 7.0 %all-to-all-start.10 = ((bf16[64,2,1792]{2,1,0:T(2,128)(2,1)}), bf16[64,2,1792]{2,1,0:T(2,128)(2,1)}, u32[]{:S(2)}, u32[]{:S(2)}) async-start(bf16[64,2,1792]{2,1,0:T(2,128)(2,1)} %reshape.452), calls=%async_computation.10 | async-start | bytes 917504 | tf_op jit(solution)/shard_map/all_to_all | solution.py:97
  469.3 65.2 %all-reduce.1 = bf16[2,64,3584]{2,1,0:T(8,128)(2,1)} all-reduce(f32[2,64,3584]{2,1,0:T(8,128)} %convolution_bitcast_fusion), channel_id=1, replica_groups=mesh['section'=8,'dp'=64] {'section'}, use_global_device_ids=true, to_apply=%region_4.5 | all-reduce | flops 458752 | bytes 2752512 | tf_op jit(solution)/shard_map/psum | solution.py:82
  534.5 1.4 convolution_select_fusion.5
  535.9 1.4 convolution_select_fusion.6
  537.4 2.1 reshape.453
  539.5 2.1 fusion.4
  (555 shorter events, 19.2 us)
Async XLA Ops:
  0.6 111.3 %copy-start = (bf16[128,3584]{1,0:T(8,128)(2,1)S(1)}, bf16[128,3584]{1,0:T(8,128)(2,1)}, u32[]{:S(2)}) copy-start(bf16[128,3584]{1,0:T(8,128)(2,1)} %param.8) | copy-start | bytes 2752516
  1.6 14.7 %copy-start.36 = (s32[192]{0:T(256)}, s32[192]{0:T(256)S(1)}, u32[]{:S(2)}) copy-start(s32[192]{0:T(256)S(1)} %reshape.417) | copy-start | bytes 2308
  22.9 14.3 %copy-start.17 = (f32[128,384]{1,0:T(8,128)S(1)}, f32[128,384]{1,0:T(8,128)}, u32[]{:S(2)}) copy-start(f32[128,384]{1,0:T(8,128)} %param.12) | copy-start | bytes 589828
  22.9 14.5 %copy-start.38 = (s32[64]{0:T(128)S(1)}, s32[64]{0:T(128)}, u32[]{:S(2)}) copy-start(s32[64]{0:T(128)} %param.11) | copy-start | bytes 772
  22.9 77.0 %all-to-all-start = ((bf16[2,192,3584]{2,0,1:T(2,128)(2,1)}), bf16[2,192,3584]{2,0,1:T(2,128)(2,1)}, u32[]{:S(2)}, u32[]{:S(2)}) async-start(bf16[2,192,3584]{2,0,1:T(2,128)(2,1)} %copy.31), calls=%async_computation | async-start | bytes 5505024 | tf_op jit(solution)/shard_map/all_to_all | solution.py:32
  111.9 3.1 copy-start.1
  115.1 17.2 %copy-start.15 = (bf16[1,64,56]{1,2,0:T(8,128)(2,1)S(1)}, bf16[1,64,56]{1,2,0:T(8,128)(2,1)}, u32[]{:S(2)}) copy-start(bf16[1,64,56]{1,2,0:T(8,128)(2,1)} %param.15) | copy-start | bytes 21508
  116.7 38.0 %copy-start.2 = (bf16[1,56,3584]{2,1,0:T(8,128)(2,1)S(1)}, bf16[1,56,3584]{2,1,0:T(8,128)(2,1)}, u32[]{:S(2)}) copy-start(bf16[1,56,3584]{2,1,0:T(8,128)(2,1)} %param.13) | copy-start | bytes 1204228
  154.7 11.3 %copy-start.6 = (bf16[64,56,64]{2,1,0:T(8,128)(2,1)}, bf16[64,56,64]{2,1,0:T(8,128)(2,1)S(1)}, u32[]{:S(2)}) copy-start(bf16[64,56,64]{2,1,0:T(8,128)(2,1)S(1)} %reshape.439) | copy-start | bytes 1376260
  155.0 2.4 copy-start.22
  155.0 7.0 %collective-permute-start = (f32[64,56]{0,1:T(8,128)S(1)}, f32[64,56]{0,1:T(8,128)S(1)}, u32[]{:S(2)}, u32[]{:S(2)}) collective-permute-start(f32[64,56]{0,1:T(8,128)S(1)} %convolution_add_fusion.7), channel_id=1, source_target_pairs={{64,0},{128,64},{192,128},{256,192},{320,256},{384,320},{448,384},... | collective-permute-start | bytes 43016 | tf_op jit(solution)/shard_map/ppermute | solution.py:12
  162.9 0.9 copy-start.7
  189.1 1.9 copy-start.24
  189.1 7.0 %collective-permute-start.1 = (f32[64,56]{0,1:T(8,128)S(1)}, f32[64,56]{0,1:T(8,128)S(1)}, u32[]{:S(2)}, u32[]{:S(2)}) collective-permute-start(f32[64,56]{0,1:T(8,128)S(1)} %convolution_add_fusion.6), channel_id=1, source_target_pairs={{64,0},{128,64},{192,128},{256,192},{320,256},{384,320},{448,384},... | collective-permute-start | bytes 43016 | tf_op jit(solution)/shard_map/ppermute | solution.py:12
  196.9 0.9 copy-start.8
  224.5 8.8 %copy-start.26 = (f32[64,56]{0,1:T(8,128)}, f32[64,56]{0,1:T(8,128)S(1)}, u32[]{:S(2)}) copy-start(f32[64,56]{0,1:T(8,128)S(1)} %convolution_add_fusion.5) | copy-start | bytes 43012
  224.6 7.0 %collective-permute-start.2 = (f32[64,56]{0,1:T(8,128)S(1)}, f32[64,56]{0,1:T(8,128)S(1)}, u32[]{:S(2)}, u32[]{:S(2)}) collective-permute-start(f32[64,56]{0,1:T(8,128)S(1)} %convolution_add_fusion.5), channel_id=1, source_target_pairs={{64,0},{128,64},{192,128},{256,192},{320,256},{384,320},{448,384},... | collective-permute-start | bytes 43016 | tf_op jit(solution)/shard_map/ppermute | solution.py:12
  232.4 0.9 copy-start.9
  262.7 8.8 %copy-start.28 = (f32[64,56]{0,1:T(8,128)}, f32[64,56]{0,1:T(8,128)S(1)}, u32[]{:S(2)}) copy-start(f32[64,56]{0,1:T(8,128)S(1)} %convolution_add_fusion.4) | copy-start | bytes 43012
  262.7 7.0 %collective-permute-start.3 = (f32[64,56]{0,1:T(8,128)S(1)}, f32[64,56]{0,1:T(8,128)S(1)}, u32[]{:S(2)}, u32[]{:S(2)}) collective-permute-start(f32[64,56]{0,1:T(8,128)S(1)} %convolution_add_fusion.4), channel_id=1, source_target_pairs={{64,0},{128,64},{192,128},{256,192},{320,256},{384,320},{448,384},... | collective-permute-start | bytes 43016 | tf_op jit(solution)/shard_map/ppermute | solution.py:12
  270.5 0.9 copy-start.10
  301.2 8.8 %copy-start.30 = (f32[64,56]{0,1:T(8,128)}, f32[64,56]{0,1:T(8,128)S(1)}, u32[]{:S(2)}) copy-start(f32[64,56]{0,1:T(8,128)S(1)} %convolution_add_fusion.3) | copy-start | bytes 43012
  301.2 7.0 %collective-permute-start.4 = (f32[64,56]{0,1:T(8,128)S(1)}, f32[64,56]{0,1:T(8,128)S(1)}, u32[]{:S(2)}, u32[]{:S(2)}) collective-permute-start(f32[64,56]{0,1:T(8,128)S(1)} %convolution_add_fusion.3), channel_id=1, source_target_pairs={{64,0},{128,64},{192,128},{256,192},{320,256},{384,320},{448,384},... | collective-permute-start | bytes 43016 | tf_op jit(solution)/shard_map/ppermute | solution.py:12
  309.1 1.0 copy-start.11
  312.9 22.3 %all-to-all-start.8 = ((bf16[64,2,1792]{2,1,0:T(2,128)(2,1)}), bf16[64,2,1792]{2,1,0:T(2,128)(2,1)}, u32[]{:S(2)}, u32[]{:S(2)}) async-start(bf16[64,2,1792]{2,1,0:T(2,128)(2,1)} %reshape.448), calls=%async_computation.8 | async-start | bytes 917504 | tf_op jit(solution)/shard_map/all_to_all | solution.py:97
  335.2 89.6 %all-to-all-start.1 = ((bf16[128,3,3584]{2,1,0:T(4,128)(2,1)}), bf16[128,3,3584]{2,1,0:T(4,128)(2,1)}, u32[]{:S(2)}, u32[]{:S(2)}) async-start(bf16[128,3,3584]{2,1,0:T(4,128)(2,1)} %copy.35), calls=%async_computation.1 | async-start | bytes 7340032 | tf_op jit(solution)/shard_map/all_to_all | solution.py:70
  346.4 9.6 %copy-start.32 = (f32[64,56]{0,1:T(8,128)}, f32[64,56]{0,1:T(8,128)S(1)}, u32[]{:S(2)}) copy-start(f32[64,56]{0,1:T(8,128)S(1)} %convolution_add_fusion.2) | copy-start | bytes 43012
  346.4 7.0 %collective-permute-start.5 = (f32[64,56]{0,1:T(8,128)S(1)}, f32[64,56]{0,1:T(8,128)S(1)}, u32[]{:S(2)}, u32[]{:S(2)}) collective-permute-start(f32[64,56]{0,1:T(8,128)S(1)} %convolution_add_fusion.2), channel_id=1, source_target_pairs={{64,0},{128,64},{192,128},{256,192},{320,256},{384,320},{448,384},... | collective-permute-start | bytes 43016 | tf_op jit(solution)/shard_map/ppermute | solution.py:12
  353.4 2.6 copy-start.20
  355.0 1.0 copy-start.12
  424.9 23.4 %all-to-all-start.9 = ((bf16[64,2,1792]{2,1,0:T(2,128)(2,1)}), bf16[64,2,1792]{2,1,0:T(2,128)(2,1)}, u32[]{:S(2)}, u32[]{:S(2)}) async-start(bf16[64,2,1792]{2,1,0:T(2,128)(2,1)} %reshape.450), calls=%async_computation.9 | async-start | bytes 917504 | tf_op jit(solution)/shard_map/all_to_all | solution.py:97
  432.9 2.9 copy-start.3
  433.0 2.9 copy-start.14
  433.0 3.6 copy-start.4
  437.2 13.1 %copy-start.21 = (f32[64,56]{0,1:T(8,128)S(1)}, f32[64,56]{0,1:T(8,128)}, u32[]{:S(2)}) copy-start(f32[64,56]{0,1:T(8,128)} %copy-done.20) | copy-start | bytes 43012
  443.2 9.4 %copy-start.37 = (s32[192]{0:T(256)S(1)}, s32[192]{0:T(256)}, u32[]{:S(2)}) copy-start(s32[192]{0:T(256)} %copy-done.36) | copy-start | bytes 2308
  450.4 7.3 %copy-start.16 = (bf16[1,64,56]{1,2,0:T(8,128)(2,1)S(1)}, bf16[1,64,56]{1,2,0:T(8,128)(2,1)}, u32[]{:S(2)}) copy-start(bf16[1,64,56]{1,2,0:T(8,128)(2,1)} %param.15) | copy-start | bytes 21508
  450.7 7.4 %copy-start.34 = (f32[64,56]{0,1:T(8,128)}, f32[64,56]{0,1:T(8,128)S(1)}, u32[]{:S(2)}) copy-start(f32[64,56]{0,1:T(8,128)S(1)} %convolution_add_fusion.1) | copy-start | bytes 43012
  450.7 7.0 %collective-permute-start.6 = (f32[64,56]{0,1:T(8,128)S(1)}, f32[64,56]{0,1:T(8,128)S(1)}, u32[]{:S(2)}, u32[]{:S(2)}) collective-permute-start(f32[64,56]{0,1:T(8,128)S(1)} %convolution_add_fusion.1), channel_id=1, source_target_pairs={{64,0},{128,64},{192,128},{256,192},{320,256},{384,320},{448,384},... | collective-permute-start | bytes 43016 | tf_op jit(solution)/shard_map/ppermute | solution.py:12
  457.7 1.8 copy-start.18
  458.3 76.2 %copy-start.5 = (bf16[64,56,64]{2,1,0:T(8,128)(2,1)S(1)}, bf16[64,56,64]{2,1,0:T(8,128)(2,1)}, u32[]{:S(2)}) copy-start(bf16[64,56,64]{2,1,0:T(8,128)(2,1)} %reshape.449) | copy-start | bytes 1376260
  458.6 0.9 copy-start.13
  462.3 75.0 %all-to-all-start.10 = ((bf16[64,2,1792]{2,1,0:T(2,128)(2,1)}), bf16[64,2,1792]{2,1,0:T(2,128)(2,1)}, u32[]{:S(2)}, u32[]{:S(2)}) async-start(bf16[64,2,1792]{2,1,0:T(2,128)(2,1)} %reshape.452), calls=%async_computation.10 | async-start | bytes 917504 | tf_op jit(solution)/shard_map/all_to_all | solution.py:97
  537.3 4.3 copy-start.19
  537.3 4.3 copy-start.23
  537.3 4.3 copy-start.25
  537.3 4.3 copy-start.27
  537.3 4.3 copy-start.29
  537.3 4.3 copy-start.31
  537.3 4.3 copy-start.33
  537.3 4.3 copy-start.35
